TPU v7x, 512 devices: a whole 4x8x8 slice. The times are simulated.
512 devices in a mesh: dp: 8 (over z), expert: 64 (over y, x, core).
Axes of the slice: x: 4, y: 8, z: 8, core: 2. Of those that a mesh axis runs over, the one named last changes fastest.
Arguments:
- tokens: bfloat16 [65536, 1024], P(('dp', 'expert')), may hold values from -6 to 6
- expert_ids: int32 [65536, 4], P(('dp', 'expert')), may hold values from 0 to 63, all different within a row; in each aligned block of 128 rows (0 to 127, 128 to 255, ...) at most 16 rows name the same one
- gate_probs: float32 [65536, 4], P(('dp', 'expert')), may hold values from 0.05 to 1
- gate_up: bfloat16 [64, 1024, 768], P('expert', 'dp'), may hold values from -0.1875 to 0.1875
- down_proj: bfloat16 [64, 384, 1024], P('expert', None, 'dp'), may hold values from -0.3125 to 0.3125
- cotangent: bfloat16 [65536, 1024], P(('dp', 'expert')), may hold values from -0.75 to 0.75
Outputs:
- moe_out: bfloat16 [65536, 1024], P(('dp', 'expert'))
- token_grads: bfloat16 [65536, 1024], P(('dp', 'expert'))
- gate_grads: float32 [65536, 4], P(('dp', 'expert'))
- gate_up_grads: float32 [64, 1024, 768], P('expert', 'dp')
- down_grads: float32 [64, 384, 1024], P('expert', None, 'dp')
Inputs may be any that keep to these rules, and one draw needn't show every extreme that they name: `expert_ids`: each row names 4 different experts. Among the rows of one device no expert is named more than 16 times, and in every draw some device names some expert exactly 16 times.
All inputs are finite; a program needn't handle non-finite values.
Results may differ from a plain program's by a relative error of at most 0.012.
Values may be sent and summed in bfloat16 or wider, within the bound.
No kernel may reach another device: no remote copies, remote signals or barrier semaphores. Data moves between devices by JAX's collectives and lax.ppermute only.
A program may use at most 64 MiB of HBM per device.

v0:
```python
import jax
import jax.numpy as jnp
from jax import lax
from jax.sharding import PartitionSpec as P


def forward_rows(rows_in, weight_in, weight_out):
    hidden_width = weight_out.shape[0]
    pre_act = jnp.dot(rows_in, weight_in, preferred_element_type=jnp.float32)
    hidden = (jax.nn.silu(pre_act[:, :hidden_width]) * pre_act[:, hidden_width:]).astype(
        jnp.bfloat16
    )
    expert_out = jnp.dot(hidden, weight_out, preferred_element_type=jnp.float32).astype(
        jnp.bfloat16
    )
    return (expert_out, pre_act, hidden)


def backward_rows(rows_in, grad_rows, pre_act, hidden, weight_in, weight_out):
    hidden_width = weight_out.shape[0]
    contract_last = (((1,), (1,)), ((), ()))
    contract_first = (((0,), (0,)), ((), ()))
    grad_hidden = lax.dot_general(
        grad_rows, weight_out, contract_last, preferred_element_type=jnp.float32
    )
    pre_gate = pre_act[:, :hidden_width]
    sigmoid_value = jax.nn.sigmoid(pre_gate)
    grad_gate = (
        grad_hidden
        * pre_act[:, hidden_width:]
        * sigmoid_value
        * (1.0 + pre_gate * (1.0 - sigmoid_value))
    )
    grad_up = grad_hidden * jax.nn.silu(pre_gate)
    grad_pre = jnp.concatenate([grad_gate, grad_up], axis=1).astype(jnp.bfloat16)
    grad_in = lax.dot_general(
        grad_pre, weight_in, contract_last, preferred_element_type=jnp.float32
    ).astype(jnp.bfloat16)
    weight_in_grad = lax.dot_general(
        rows_in, grad_pre, contract_first, preferred_element_type=jnp.float32
    )
    weight_out_grad = lax.dot_general(
        hidden, grad_rows, contract_first, preferred_element_type=jnp.float32
    )
    return (grad_in, weight_in_grad, weight_out_grad)


def live_slots(recv_counts, capacity):
    within = jnp.arange(capacity, dtype=jnp.int32)[None, :] < recv_counts[:, None]
    return within.reshape(-1)


def expert_forward(rows_in, filled, weight_in, weight_out):
    zero_row = jnp.zeros((), jnp.bfloat16)
    expert_out, pre_act, hidden = forward_rows(rows_in, weight_in, weight_out)
    expert_out = jnp.where(filled[:, None], expert_out, zero_row)
    stored = (rows_in, pre_act, hidden, None)
    return (expert_out, stored)


def expert_backward(grads_in, filled, stored, weight_in, weight_out):
    zero_row = jnp.zeros((), jnp.bfloat16)
    rows_in, pre_act, hidden, unused_plan = stored
    grad_back, in_grad, out_grad = backward_rows(
        rows_in, grads_in, pre_act, hidden, weight_in, weight_out
    )
    grad_back = jnp.where(filled[:, None], grad_back, zero_row)
    return (grad_back, in_grad, out_grad)


def local(tokens, expert_ids, gate_probs, gate_up, down_proj, cotangent):
    token_count, top_count = expert_ids.shape
    expert_count = lax.axis_size("expert")
    capacity = 2 * token_count * top_count // expert_count
    route_count = token_count * top_count
    slot_count = expert_count * capacity
    flat_ids = expert_ids.reshape(route_count)
    onehot = (flat_ids[:, None] == jnp.arange(expert_count, dtype=jnp.int32)[None, :]).astype(
        jnp.int32
    )
    slot_index = jnp.sum((jnp.cumsum(onehot, axis=0) - onehot) * onehot, axis=1)
    position = flat_ids * capacity + slot_index
    counts = jnp.sum(onehot, axis=0)
    slot_range = jnp.arange(slot_count, dtype=jnp.int32)
    matches = position[None, :] == slot_range[:, None]
    route_of_slot = jnp.sum(
        jnp.where(matches, jnp.arange(route_count, dtype=jnp.int32)[None, :], 0), axis=1
    )
    slot_filled = jnp.any(matches, axis=1)
    token_of_slot = route_of_slot // top_count
    zero_row = jnp.zeros((), jnp.bfloat16)
    send_tokens = jnp.where(slot_filled[:, None], tokens[token_of_slot], zero_row)
    slot_probs = jnp.where(slot_filled, gate_probs.reshape(route_count)[route_of_slot], 0.0)
    send_grads = (slot_probs[:, None] * cotangent[token_of_slot].astype(jnp.float32)).astype(
        jnp.bfloat16
    )
    weight_in, weight_out = (
        lax.all_gather(gate_up, "dp", axis=1, tiled=True),
        lax.all_gather(down_proj, "dp", axis=2, tiled=True),
    )
    weight_in = weight_in[0]
    weight_out = weight_out[0]
    rows_in, recv_counts = (
        lax.all_to_all(send_tokens, "expert", split_axis=0, concat_axis=0, tiled=True),
        lax.all_to_all(counts, "expert", split_axis=0, concat_axis=0, tiled=True),
    )
    filled = live_slots(recv_counts, capacity)
    expert_out, stored = expert_forward(rows_in, filled, weight_in, weight_out)
    back_out = lax.all_to_all(expert_out, "expert", split_axis=0, concat_axis=0, tiled=True)
    grads_in = lax.all_to_all(send_grads, "expert", split_axis=0, concat_axis=0, tiled=True)
    grad_back, in_grad, out_grad = expert_backward(grads_in, filled, stored, weight_in, weight_out)
    back_grad = lax.all_to_all(grad_back, "expert", split_axis=0, concat_axis=0, tiled=True)
    sum_in, sum_out = (
        lax.psum_scatter(
            in_grad[None].astype(jnp.bfloat16), "dp", scatter_dimension=1, tiled=True
        ).astype(jnp.float32),
        lax.psum_scatter(
            out_grad[None].astype(jnp.bfloat16), "dp", scatter_dimension=2, tiled=True
        ).astype(jnp.float32),
    )
    out_routes = back_out[position].reshape(token_count, top_count, -1).astype(jnp.float32)
    moe_out = jnp.sum(gate_probs[:, :, None] * out_routes, axis=1).astype(jnp.bfloat16)
    gate_grads = jnp.sum(cotangent.astype(jnp.float32)[:, None, :] * out_routes, axis=2)
    grad_routes = back_grad[position].reshape(token_count, top_count, -1).astype(jnp.float32)
    token_grads = jnp.sum(grad_routes, axis=1).astype(jnp.bfloat16)
    return (moe_out, token_grads, gate_grads, sum_in, sum_out)


def solution(mesh):
    return jax.shard_map(
        local,
        mesh=mesh,
        in_specs=(
            P(("dp", "expert"), None),
            P(("dp", "expert"), None),
            P(("dp", "expert"), None),
            P("expert", "dp", None),
            P("expert", None, "dp"),
            P(("dp", "expert"), None),
        ),
        out_specs=(
            P(("dp", "expert"), None),
            P(("dp", "expert"), None),
            P(("dp", "expert"), None),
            P("expert", "dp", None),
            P("expert", None, "dp"),
        ),
        check_vma=False,
    )
```

profile of v0, /device:TPU:2, one launch (start us, length us, event | category | flops | bytes accessed | tf_op | source)
XLA Modules:
  0.0 300.2 jit_solution(8653985739572995588)
XLA Ops:
  7.2 0.0 copy-start
  7.2 0.8 copy.35
  8.0 0.1 eq.42
  8.1 0.1 eq.38
  8.2 1.2 reduce-window.6
  9.5 0.2 slice_reduce_fusion
  9.7 0.2 fusion.12
  9.9 0.7 copy.36
  10.6 10.7 %all-to-all-start = ((s32[64,1,1]{2,1,0:T(1,128)}), s32[64,1,1]{2,1,0:T(1,128)S(1)}, u32[]{:S(2)}, u32[]{:S(2)}) async-start(s32[64,1,1]{2,1,0:T(1,128)} %copy.36), calls=%async_computation | async-start | bytes 65536 | tf_op jit(solution)/shard_map/all_to_all | solution.py:105
  21.3 0.3 select_reduce_fusion
  21.6 0.3 fusion.1
  21.9 0.1 broadcast_in_dim.60
  22.0 4.1 %gather_fusion = bf16[1024,1024]{1,0:T(8,128)(2,1)S(1)} fusion(bf16[128,1024]{1,0:T(8,128)(2,1)S(1)} %copy-done, s32[1024]{0:T(1024)S(1)} %broadcast_clamp_fusion.1), kind=kCustom, calls=%fused_computation | custom fusion | bytes 4198400 | tf_op jit(solution)/shard_map/gather | solution.py:92
  26.1 1.6 broadcast_select_fusion
  27.7 2.2 all-to-all-done
  29.8 8.5 %all-to-all-start.1 = ((bf16[64,16,1024]{2,1,0:T(8,128)(2,1)}), bf16[64,16,1024]{2,1,0:T(8,128)(2,1)}, u32[]{:S(2)}, u32[]{:S(2)}) async-start(bf16[64,16,1024]{2,1,0:T(8,128)(2,1)} %broadcast_select_fusion), calls=%async_computation.1 | async-start | bytes 4194304 | tf_op jit(solution)/shard_map/all_to_all | solution.py:104
  38.3 0.1 copy.34
  38.4 0.1 reshape.204
  38.5 0.0 copy-start.1
  38.5 6.9 %gather_fusion.2 = f32[1024]{0:T(1024)S(1)} fusion(f32[512]{0:T(512)S(1)} %reshape.204, s32[1024]{0:T(1024)S(1)} %broadcast_clamp_fusion), kind=kCustom, calls=%fused_computation.2 | custom fusion | bytes 12288 | tf_op jit(solution)/shard_map/gather | solution.py:93
  45.4 0.1 gather.23
  45.5 4.1 %gather_fusion.3 = bf16[1024,1024]{1,0:T(8,128)(2,1)S(1)} fusion(bf16[128,1024]{1,0:T(8,128)(2,1)S(1)} %copy-done.1, s32[1024]{0:T(1024)S(1)} %broadcast_clamp_fusion.1), kind=kCustom, calls=%fused_computation.3 | custom fusion | bytes 4198400 | tf_op jit(solution)/shard_map/gather | solution.py:94
  49.6 1.8 fusion
  51.4 38.1 %all-to-all-done.1 = bf16[64,16,1024]{2,1,0:T(8,128)(2,1)} async-done(((bf16[64,16,1024]{2,1,0:T(8,128)(2,1)}), bf16[64,16,1024]{2,1,0:T(8,128)(2,1)}, u32[]{:S(2)}, u32[]{:S(2)}) %all-to-all-start.1) | async-done | bytes 2097184 | tf_op jit(solution)/shard_map/all_to_all | solution.py:104
  89.4 5.4 %all-to-all-start.3 = ((bf16[64,16,1024]{2,1,0:T(8,128)(2,1)}), bf16[64,16,1024]{2,1,0:T(8,128)(2,1)S(1)}, u32[]{:S(2)}, u32[]{:S(2)}) async-start(bf16[64,16,1024]{2,1,0:T(8,128)(2,1)} %fusion), calls=%async_computation.3 | async-start | bytes 4194304 | tf_op jit(solution)/shard_map/all_to_all | solution.py:110
  94.9 0.0 all-gather.2.cloned.1.call-start
  94.9 0.7 all-gather.2.cloned.1.call-update
  95.6 34.6 %all_gather.7 = bf16[1,384,1024]{2,1,0:T(8,128)(2,1)S(1)} all-gather(bf16[1,384,128]{2,1,0:T(8,128)(2,1)} %param.10), channel_id=1, replica_groups=mesh['dp'=8,'expert'=64] {'dp'}, dimensions={2}, use_global_device_ids=true | all-gather | bytes 884736 | tf_op jit(solution)/shard_map/all_gather | solution.py:99
  130.2 1.2 reduce.5
  131.4 0.1 iota_compare_fusion.3
  131.5 0.1 lt.50
  131.6 15.3 %all-gather.2.cloned.1.call-done = bf16[1,1024,768]{2,1,0:T(8,128)(2,1)} async-done(((bf16[1,128,768]{2,1,0:T(8,128)(2,1)}), bf16[1,1024,768]{2,1,0:T(8,128)(2,1)}) %all-gather.2.cloned.1.call-update) | async-done | bytes 1572880 | tf_op jit(solution)/shard_map/all_gather | solution.py:98
  146.9 5.5 %fusion.3 = f32[1024,768]{0,1:T(8,128)} fusion(bf16[1024,1024]{1,0:T(8,128)(2,1)} %bitcast.5, bf16[1,1024,768]{2,1,0:T(8,128)(2,1)} %all-gather.2.cloned.1.call-done), kind=kOutput, calls=%fused_computation.18 | convolution fusion | flops 1610612736 | bytes 6815744 | tf_op jit(solution)/shard_map/dot_general | solution.py:9
  152.5 0.0 all-to-all-done.3
  152.5 5.1 %multiply_convert_fusion.1 = (bf16[1024,384]{0,1:T(8,128)(2,1)S(1)}, bf16[1024,384]{0,1:T(8,128)(2,1)S(1)}, bf16[1024,384]{0,1:T(8,128)(2,1)}) fusion(f32[1024,768]{0,1:T(8,128)} %fusion.3, bf16[1024,1024]{1,0:T(8,128)(2,1)S(1)} %bitcast.60, bf16[1,384,1024]{2,1,0:T(8,128)(2,1)S(1)} %all_gather.7), kind=kOutput, calls=%fused_computation.21 | convolution fusion | flops 811204608 | bytes 8388608 | tf_op jit(solution)/shard_map/dot_general | solution.py:23
  157.6 3.3 %convert_select_fusion = bf16[1024,1024]{1,0:T(8,128)(2,1)} fusion(pred[1024]{0:T(1024)(128)(4,1)S(1)} %lt.50, bf16[1,1024,768]{2,1,0:T(8,128)(2,1)S(1)} %copy-done.6, bf16[1024,384]{0,1:T(8,128)(2,1)S(1)} %get-tuple-element.25, bf16[1024,384]{0,1:T(8,128)(2,1)S(1)} %get-tuple-element.24), kind=kOutput, calls=%fused_computation.8 | convolution fusion | flops 1615855616 | bytes 5243904 | tf_op jit(solution)/shard_map/dot_general | solution.py:36
  160.9 10.3 %all-to-all-start.4 = ((bf16[64,16,1024]{2,1,0:T(8,128)(2,1)}), bf16[64,16,1024]{2,1,0:T(8,128)(2,1)S(1)}, u32[]{:S(2)}, u32[]{:S(2)}) async-start(bf16[64,16,1024]{2,1,0:T(8,128)(2,1)} %bitcast.62), calls=%async_computation.4 | async-start | bytes 4194304 | tf_op jit(solution)/shard_map/all_to_all | solution.py:112
  171.2 0.0 reduce-scatter.7.cloned.1.call-start
  171.2 3.7 %fusion.7 = bf16[1,384,1024]{2,1,0:T(8,128)(2,1)} fusion(bf16[1024,384]{0,1:T(8,128)(2,1)} %get-tuple-element.26, bf16[1024,1024]{1,0:T(8,128)(2,1)} %bitcast.61), kind=kOutput, calls=%fused_computation.27 | convolution fusion | flops 805699584 | bytes 3670016 | tf_op jit(solution)/shard_map/dot_general | solution.py:42
  174.9 4.8 %copy.42 = bf16[1,384,1024]{1,0,2:T(2,128)(2,1)} copy(bf16[1,384,1024]{2,1,0:T(8,128)(2,1)} %fusion.7) | data formatting | bytes 1572864
  179.7 2.5 copy.48
  182.2 0.0 reduce-scatter.7.cloned.1.call-update
  182.3 3.8 %convert_select_fusion.1 = bf16[1024,1024]{1,0:T(8,128)(2,1)} fusion(pred[1024]{0:T(1024)(128)(4,1)S(1)} %lt.50, bf16[1024,384]{0,1:T(8,128)(2,1)} %get-tuple-element.26, bf16[1,384,1024]{2,1,0:T(8,128)(2,1)S(1)} %all_gather.7), kind=kOutput, calls=%fused_computation.10 | convolution fusion | flops 807403520 | bytes 3671040 | tf_op jit(solution)/shard_map/dot_general | solution.py:13
  186.0 36.4 %all-to-all-done.4 = bf16[64,16,1024]{2,1,0:T(8,128)(2,1)S(1)} async-done(((bf16[64,16,1024]{2,1,0:T(8,128)(2,1)}), bf16[64,16,1024]{2,1,0:T(8,128)(2,1)S(1)}, u32[]{:S(2)}, u32[]{:S(2)}) %all-to-all-start.4) | async-done | bytes 2097184 | tf_op jit(solution)/shard_map/all_to_all | solution.py:112
  222.4 5.8 %all-to-all-start.2 = ((bf16[64,16,1024]{2,1,0:T(8,128)(2,1)}), bf16[64,16,1024]{2,1,0:T(8,128)(2,1)}, u32[]{:S(2)}, u32[]{:S(2)}) async-start(bf16[64,16,1024]{2,1,0:T(8,128)(2,1)} %bitcast.59), calls=%async_computation.2 | async-start | bytes 4194304 | tf_op jit(solution)/shard_map/all_to_all | solution.py:109
  228.2 0.3 reduce-scatter.5.cloned.1.call-start
  228.5 4.8 %fusion.6 = bf16[1,1024,768]{2,1,0:T(8,128)(2,1)} fusion(bf16[1024,1024]{1,0:T(8,128)(2,1)} %bitcast.5, bf16[1024,384]{0,1:T(8,128)(2,1)} %copy-done.9, bf16[1024,384]{0,1:T(8,128)(2,1)S(1)} %copy-done.8), kind=kOutput, calls=%fused_computation.25 | convolution fusion | flops 1614544896 | bytes 5242880 | tf_op jit(solution)/shard_map/dot_general | solution.py:39
  233.3 0.0 reduce-scatter.5.cloned.1.call-update
  233.3 0.8 convert_element_type.75
  234.2 0.1 copy.39
  234.3 0.1 mul.87
  234.4 0.0 reduce-scatter.7.cloned.1.call-done
  234.5 1.0 reshape_bitcast_fusion
  235.5 0.2 copy.43
  235.6 0.7 convert_element_type.81
  236.3 38.8 %reduce-scatter.5.cloned.1.call-done = bf16[1,128,768]{2,1,0:T(8,128)(2,1)} async-done(((bf16[1,1024,768]{2,1,0:T(8,128)(2,1)}), bf16[1,128,768]{2,1,0:T(8,128)(2,1)}) %reduce-scatter.5.cloned.1.call-update) | async-done | bytes 196624 | tf_op jit(solution)/shard_map/reduce_scatter | solution.py:114
  275.1 1.7 convert_element_type.78
  276.8 2.8 gather_fusion.4
  279.6 2.3 reshape.205
  281.9 4.6 %gather_fusion.1 = bf16[512,1024]{1,0:T(8,128)(2,1)S(1)} fusion(bf16[1024,1024]{1,0:T(8,128)(2,1)} %bitcast.9, s32[1024]{0:T(1024)S(1)} %pad_clamp_fusion), kind=kCustom, calls=%fused_computation.1 | custom fusion | bytes 2099200 | tf_op jit(solution)/shard_map/gather | solution.py:121
  286.5 0.7 reshape.206
  287.2 3.7 %multiply_reduce_fusion = (f32[128,4]{1,0:T(8,128)S(1)}, bf16[128,1024]{1,0:T(8,128)(2,1)}) fusion(f32[128,4,1024]{2,1,0:T(4,128)S(1)} %reshape.206, f32[128,1024]{1,0:T(8,128)} %convert_element_type.75, f32[128,4]{1,0:T(8,128)S(1)} %copy.34), kind=kLoop, calls=%fused_computation.7 | loop fusion | flops 1965568 | bytes 2887680 | tf_op jit(solution)/shard_map/reduce_sum | solution.py:123
  290.9 0.7 copy.41
  291.5 2.1 reduce_sum.67
  (30 shorter events, 0.2 us)
Async XLA Ops:
  7.2 14.8 %copy-start = (bf16[128,1024]{1,0:T(8,128)(2,1)S(1)}, bf16[128,1024]{1,0:T(8,128)(2,1)}, u32[]{:S(2)}) copy-start(bf16[128,1024]{1,0:T(8,128)(2,1)} %param.6) | copy-start | bytes 786436
  10.6 19.2 %all-to-all-start = ((s32[64,1,1]{2,1,0:T(1,128)}), s32[64,1,1]{2,1,0:T(1,128)S(1)}, u32[]{:S(2)}, u32[]{:S(2)}) async-start(s32[64,1,1]{2,1,0:T(1,128)} %copy.36), calls=%async_computation | async-start | bytes 65536 | tf_op jit(solution)/shard_map/all_to_all | solution.py:105
  27.7 10.6 %copy-start.5 = (f32[128,4]{0,1:T(4,128)S(1)}, f32[128,4]{0,1:T(4,128)}, u32[]{:S(2)}) copy-start(f32[128,4]{0,1:T(4,128)} %param.8) | copy-start | bytes 6148
  29.8 59.6 %all-to-all-start.1 = ((bf16[64,16,1024]{2,1,0:T(8,128)(2,1)}), bf16[64,16,1024]{2,1,0:T(8,128)(2,1)}, u32[]{:S(2)}, u32[]{:S(2)}) async-start(bf16[64,16,1024]{2,1,0:T(8,128)(2,1)} %broadcast_select_fusion), calls=%async_computation.1 | async-start | bytes 4194304 | tf_op jit(solution)/shard_map/all_to_all | solution.py:104
  38.5 7.0 %copy-start.1 = (bf16[128,1024]{1,0:T(8,128)(2,1)S(1)}, bf16[128,1024]{1,0:T(8,128)(2,1)}, u32[]{:S(2)}) copy-start(bf16[128,1024]{1,0:T(8,128)(2,1)} %param.11) | copy-start | bytes 786436
  89.4 63.0 %all-to-all-start.3 = ((bf16[64,16,1024]{2,1,0:T(8,128)(2,1)}), bf16[64,16,1024]{2,1,0:T(8,128)(2,1)S(1)}, u32[]{:S(2)}, u32[]{:S(2)}) async-start(bf16[64,16,1024]{2,1,0:T(8,128)(2,1)} %fusion), calls=%async_computation.3 | async-start | bytes 4194304 | tf_op jit(solution)/shard_map/all_to_all | solution.py:110
  94.9 52.0 %all-gather.2.cloned.1.call-start = ((), (), s32[]{:S(2)}) async-start(), calls=%async_computation.7 | async-start | bytes 1769472 | tf_op jit(solution)/shard_map/all_gather | solution.py:98
  152.5 5.1 %copy-start.3 = (bf16[64,16,1024]{2,1,0:T(8,128)(2,1)}, bf16[64,16,1024]{2,1,0:T(8,128)(2,1)S(1)}, u32[]{:S(2)}) copy-start(bf16[64,16,1024]{2,1,0:T(8,128)(2,1)S(1)} %all-to-all-done.3) | copy-start | bytes 6291460
  152.5 5.1 %copy-start.6 = (bf16[1,1024,768]{2,1,0:T(8,128)(2,1)S(1)}, bf16[1,1024,768]{2,1,0:T(8,128)(2,1)}, u32[]{:S(2)}) copy-start(bf16[1,1024,768]{2,1,0:T(8,128)(2,1)} %all-gather.2.cloned.1.call-done) | copy-start | bytes 4718596
  157.6 3.3 %copy-start.7 = (bf16[1024,384]{0,1:T(8,128)(2,1)}, bf16[1024,384]{0,1:T(8,128)(2,1)S(1)}, u32[]{:S(2)}) copy-start(bf16[1024,384]{0,1:T(8,128)(2,1)S(1)} %get-tuple-element.24) | copy-start | bytes 2359300
  157.6 3.3 %copy-start.9 = (bf16[1024,384]{0,1:T(8,128)(2,1)}, bf16[1024,384]{0,1:T(8,128)(2,1)S(1)}, u32[]{:S(2)}) copy-start(bf16[1024,384]{0,1:T(8,128)(2,1)S(1)} %get-tuple-element.25) | copy-start | bytes 2359300
  160.9 61.5 %all-to-all-start.4 = ((bf16[64,16,1024]{2,1,0:T(8,128)(2,1)}), bf16[64,16,1024]{2,1,0:T(8,128)(2,1)S(1)}, u32[]{:S(2)}, u32[]{:S(2)}) async-start(bf16[64,16,1024]{2,1,0:T(8,128)(2,1)} %bitcast.62), calls=%async_computation.4 | async-start | bytes 4194304 | tf_op jit(solution)/shard_map/all_to_all | solution.py:112
  171.2 63.3 %reduce-scatter.7.cloned.1.call-start = ((), (), s32[]{:S(2)}) async-start(), calls=%async_computation.9 | async-start | bytes 884736
  222.4 6.0 %copy-start.8 = (bf16[1024,384]{0,1:T(8,128)(2,1)S(1)}, bf16[1024,384]{0,1:T(8,128)(2,1)}, u32[]{:S(2)}) copy-start(bf16[1024,384]{0,1:T(8,128)(2,1)} %copy-done.7) | copy-start | bytes 2359300
  222.4 59.4 %all-to-all-start.2 = ((bf16[64,16,1024]{2,1,0:T(8,128)(2,1)}), bf16[64,16,1024]{2,1,0:T(8,128)(2,1)}, u32[]{:S(2)}, u32[]{:S(2)}) async-start(bf16[64,16,1024]{2,1,0:T(8,128)(2,1)} %bitcast.59), calls=%async_computation.2 | async-start | bytes 4194304 | tf_op jit(solution)/shard_map/all_to_all | solution.py:109
  228.2 46.9 %reduce-scatter.5.cloned.1.call-start = ((), (), s32[]{:S(2)}) async-start(), calls=%async_computation.8 | async-start | bytes 1769472 | tf_op jit(solution)/shard_map/reduce_scatter | solution.py:114
  233.3 0.9 copy-start.4
  287.2 4.4 %copy-start.2 = (bf16[128,4,1024]{2,1,0:T(4,128)(2,1)S(1)}, bf16[128,4,1024]{2,1,0:T(4,128)(2,1)}, u32[]{:S(2)}) copy-start(bf16[128,4,1024]{2,1,0:T(4,128)(2,1)} %reshape.205) | copy-start | bytes 3145732
Sparse Core Ops, SparseCore 0:
  97.8 49.0 all-gather.1
  182.4 39.1 reduce-scatter.6
  233.4 41.6 reduce-scatter.4
where the time goes:
time: 301 us; the launch traced here: 300 us
  waiting for transfers between devices  131 us (44%)
  starting transfers between devices  40.9 us (14%)
  local copies, waits for them, and re-layouts  37.2 us (12%)
  blocking collectives  34.6 us (11%)
  matrix products  26.3 us (9%)
  other arithmetic  15.8 us (5%)
  between operations  14 us (5%)
    reduce_scatter x1, waiting for transfers between devices, local(): lax.psum_scatter(in_grad[None].astype(jnp.bfloat16), 'dp', scatter_dimens...  38.8 us
    all_to_all x1, waiting for transfers between devices, local(): lax.all_to_all(send_tokens, 'expert', split_axis=0, concat_axis=0, tiled=...  38.1 us
    all_to_all x1, waiting for transfers between devices, local(): lax.all_to_all(grad_back, 'expert', split_axis=0, concat_axis=0, tiled=True)  36.4 us
    all_gather x1, blocking collectives, local(): lax.all_gather(down_proj, 'dp', axis=2, tiled=True)  34.6 us
    all_gather x1, waiting for transfers between devices, local(): lax.all_gather(gate_up, 'dp', axis=1, tiled=True)  15.3 us
    all_to_all x1, starting transfers between devices, local(): lax.all_to_all(counts, 'expert', split_axis=0, concat_axis=0, tiled=True)  10.7 us
    all_to_all x1, starting transfers between devices, local(): lax.all_to_all(grad_back, 'expert', split_axis=0, concat_axis=0, tiled=True)  10.3 us
    unnamed x27, local copies, waits for them, and re-layouts  10.1 us
  transfers between devices with their start and end apart: 8, of which 5 were waited for; matrix products, arithmetic and copies ran while one was open for 19% of the time, Pallas kernels for 0%

commit v1 on v0

--- a/solution.py
+++ b/solution.py
@@ -2,6 +2,27 @@
 import jax.numpy as jnp
 from jax import lax
 from jax.sharding import PartitionSpec as P
+
+
+def ring_gather(array, axis, dim):
+    size, index, rows = (lax.axis_size(axis), lax.axis_index(axis), array.shape[dim])
+    upward = [(i, (i + 1) % size) for i in range(size)]
+    left = [(i, (i - 1) % size) for i in range(size)]
+    result = jnp.zeros((*array.shape[:dim], size * rows, *array.shape[dim + 1 :]), array.dtype)
+    result = lax.dynamic_update_slice_in_dim(result, array, index * rows, axis=dim)
+    from_left = from_right = array
+    halfway = size // 2
+    for step in range(1, halfway + 1):
+        from_left = lax.ppermute(from_left, axis, upward)
+        result = lax.dynamic_update_slice_in_dim(
+            result, from_left, (index - step) % size * rows, axis=dim
+        )
+        if step < size - halfway:
+            from_right = lax.ppermute(from_right, axis, left)
+            result = lax.dynamic_update_slice_in_dim(
+                result, from_right, (index + step) % size * rows, axis=dim
+            )
+    return result
 
 
 def forward_rows(rows_in, weight_in, weight_out):
@@ -95,7 +116,7 @@
         jnp.bfloat16
     )
     weight_in, weight_out = (
-        lax.all_gather(gate_up, "dp", axis=1, tiled=True),
+        ring_gather(gate_up, "dp", 1),
         lax.all_gather(down_proj, "dp", axis=2, tiled=True),
     )
     weight_in = weight_in[0]

time: 301 us -> 323 us (1.073)
  starting transfers between devices: 40.9 us -> 69.7 us
  local copies, waits for them, and re-layouts: 37.2 us -> 48.3 us
  blocking collectives: 34.6 us -> 25.3 us
  waiting for transfers between devices: 131 us -> 122 us
    ppermute x0 -> x7, starting transfers between devices: none -> 29.1 us  [the longest x3 18.5 us: ring_gather(): from_right = lax.ppermute(from_right, axis, left)]
    all_gather x1 -> x0, waiting for transfers between devices: 15.3 us -> none  [local(): lax.all_gather(gate_up, 'dp', axis=1, tiled=True)]
    all_gather x1, blocking collectives: 34.6 us -> 25.3 us  [local(): lax.all_gather(down_proj, 'dp', axis=2, tiled=True)]
    dynamic_update_slice x0 -> x8, local copies, waits for them, and re-layouts: none -> 8.31 us  [the longest x4 3.7 us: ring_gather(): lax.dynamic_update_slice_in_dim(result, from_left, (index - step) % size...]
    ppermute x0 -> x7, waiting for transfers between devices: none -> 5.65 us  [the longest x4 5.64 us: ring_gather(): from_left = lax.ppermute(from_left, axis, upward)]
    unnamed x27 -> x23, local copies, waits for them, and re-layouts: 10.1 us -> 10.7 us
  transfers between devices with their start and end apart: 8 -> 14, of which waited for: 5 -> 6; matrix products, arithmetic and copies ran while one was open for 19% -> 20% of each run, Pallas kernels for 0% -> 0%
where the time goes in v1:
time: 323 us; the launch traced here: 322 us
  waiting for transfers between devices  122 us (38%)
  starting transfers between devices  69.7 us (22%)
  local copies, waits for them, and re-layouts  48.3 us (15%)
  matrix products  28.3 us (9%)
  blocking collectives  25.3 us (8%)
  between operations  14.5 us (4%)
  other arithmetic  13.8 us (4%)
    reduce_scatter x1, waiting for transfers between devices, local(): lax.psum_scatter(in_grad[None].astype(jnp.bfloat16), 'dp', scatter_dimens...  39.7 us
    all_to_all x1, waiting for transfers between devices, local(): lax.all_to_all(send_tokens, 'expert', split_axis=0, concat_axis=0, tiled=...  38.1 us
    all_to_all x1, waiting for transfers between devices, local(): lax.all_to_all(grad_back, 'expert', split_axis=0, concat_axis=0, tiled=True)  36.4 us
    all_gather x1, blocking collectives, local(): lax.all_gather(down_proj, 'dp', axis=2, tiled=True)  25.3 us
    ppermute x3, starting transfers between devices, ring_gather(): from_right = lax.ppermute(from_right, axis, left)  18.5 us
    unnamed x23, local copies, waits for them, and re-layouts  10.7 us
    all_to_all x1, starting transfers between devices, local(): lax.all_to_all(counts, 'expert', split_axis=0, concat_axis=0, tiled=True)  10.7 us
    ppermute x4, starting transfers between devices, ring_gather(): from_left = lax.ppermute(from_left, axis, upward)  10.5 us
  transfers between devices with their start and end apart: 14, of which 6 were waited for; matrix products, arithmetic and copies ran while one was open for 20% of the time, Pallas kernels for 0%

profile of v1, /device:TPU:2, one launch (start us, length us, event | category | flops | bytes accessed | tf_op | source)
XLA Modules:
  0.0 321.9 jit_solution(8610029935241159874)
XLA Ops:
  7.2 0.8 copy.35
  8.2 1.2 reduce-window.6
  9.5 0.2 slice_reduce_fusion
  9.7 0.2 fusion.9
  9.9 0.7 copy.36
  10.6 10.7 %all-to-all-start = ((s32[64,1,1]{2,1,0:T(1,128)}), s32[64,1,1]{2,1,0:T(1,128)S(1)}, u32[]{:S(2)}, u32[]{:S(2)}) async-start(s32[64,1,1]{2,1,0:T(1,128)} %copy.36), calls=%async_computation | async-start | bytes 65536 | tf_op jit(solution)/shard_map/all_to_all | solution.py:126
  21.3 0.3 select_reduce_fusion
  21.6 0.3 fusion.1
  22.0 4.1 %gather_fusion = bf16[1024,1024]{1,0:T(8,128)(2,1)S(1)} fusion(bf16[128,1024]{1,0:T(8,128)(2,1)S(1)} %copy-done, s32[1024]{0:T(1024)S(1)} %broadcast_clamp_fusion.1), kind=kCustom, calls=%fused_computation | custom fusion | bytes 4198400 | tf_op jit(solution)/shard_map/gather | solution.py:113
  26.1 1.5 broadcast_select_fusion
  27.6 2.2 all-to-all-done
  29.8 8.4 %all-to-all-start.1 = ((bf16[64,16,1024]{2,1,0:T(8,128)(2,1)}), bf16[64,16,1024]{2,1,0:T(8,128)(2,1)}, u32[]{:S(2)}, u32[]{:S(2)}) async-start(bf16[64,16,1024]{2,1,0:T(8,128)(2,1)} %broadcast_select_fusion), calls=%async_computation.1 | async-start | bytes 4194304 | tf_op jit(solution)/shard_map/all_to_all | solution.py:125
  38.3 0.1 copy.34
  38.5 6.9 %gather_fusion.2 = f32[1024]{0:T(1024)S(1)} fusion(f32[512]{0:T(512)S(1)} %reshape.220, s32[1024]{0:T(1024)S(1)} %broadcast_clamp_fusion), kind=kCustom, calls=%fused_computation.2 | custom fusion | bytes 12288 | tf_op jit(solution)/shard_map/gather | solution.py:114
  45.5 4.1 %gather_fusion.3 = bf16[1024,1024]{1,0:T(8,128)(2,1)S(1)} fusion(bf16[128,1024]{1,0:T(8,128)(2,1)S(1)} %copy-done.1, s32[1024]{0:T(1024)S(1)} %broadcast_clamp_fusion.1), kind=kCustom, calls=%fused_computation.3 | custom fusion | bytes 4198400 | tf_op jit(solution)/shard_map/gather | solution.py:115
  49.6 1.8 fusion
  51.3 38.1 %all-to-all-done.1 = bf16[64,16,1024]{2,1,0:T(8,128)(2,1)} async-done(((bf16[64,16,1024]{2,1,0:T(8,128)(2,1)}), bf16[64,16,1024]{2,1,0:T(8,128)(2,1)}, u32[]{:S(2)}, u32[]{:S(2)}) %all-to-all-start.1) | async-done | bytes 2097184 | tf_op jit(solution)/shard_map/all_to_all | solution.py:125
  89.4 5.4 %all-to-all-start.3 = ((bf16[64,16,1024]{2,1,0:T(8,128)(2,1)}), bf16[64,16,1024]{2,1,0:T(8,128)(2,1)S(1)}, u32[]{:S(2)}, u32[]{:S(2)}) async-start(bf16[64,16,1024]{2,1,0:T(8,128)(2,1)} %fusion), calls=%async_computation.3 | async-start | bytes 4194304 | tf_op jit(solution)/shard_map/all_to_all | solution.py:131
  94.9 4.3 %collective-permute-start = (bf16[1,128,768]{2,1,0:T(8,128)(2,1)}, bf16[1,128,768]{2,1,0:T(8,128)(2,1)}, u32[]{:S(2)}, u32[]{:S(2)}) collective-permute-start(bf16[1,128,768]{2,1,0:T(8,128)(2,1)} %param.9), channel_id=1, source_target_pairs={{0,64},{64,128},{128,192},{192,256},{256,320},{320,384},{384,448},... | collective-permute-start | bytes 589832 | tf_op jit(solution)/shard_map/ppermute | solution.py:16
  99.1 8.6 %collective-permute-start.1 = (bf16[1,128,768]{2,1,0:T(8,128)(2,1)}, bf16[1,128,768]{2,1,0:T(8,128)(2,1)}, u32[]{:S(2)}, u32[]{:S(2)}) collective-permute-start(bf16[1,128,768]{2,1,0:T(8,128)(2,1)} %param.9), channel_id=1, source_target_pairs={{0,448},{64,0},{128,64},{192,128},{256,192},{320,256},{384,320},{4... | collective-permute-start | bytes 589832 | tf_op jit(solution)/shard_map/ppermute | solution.py:21
  107.9 1.3 squeeze.22
  109.1 1.6 bitcast_dynamic-update-slice_fusion.7
  110.8 25.3 %all_gather.3 = bf16[1,384,1024]{2,1,0:T(8,128)(2,1)S(1)} all-gather(bf16[1,384,128]{2,1,0:T(8,128)(2,1)} %param.10), channel_id=1, replica_groups=mesh['dp'=8,'expert'=64] {'dp'}, dimensions={2}, use_global_device_ids=true | all-gather | bytes 884736 | tf_op jit(solution)/shard_map/all_gather | solution.py:120
  136.1 1.2 reduce.5
  137.5 2.2 collective-permute-start.2
  139.7 4.8 %collective-permute-start.3 = (bf16[1,128,768]{2,1,0:T(8,128)(2,1)}, bf16[1,128,768]{2,1,0:T(8,128)(2,1)S(1)}, u32[]{:S(2)}, u32[]{:S(2)}) collective-permute-start(bf16[1,128,768]{2,1,0:T(8,128)(2,1)} %collective-permute-done.1), channel_id=1, source_target_pairs={{0,448},{64,0},{128,64},{192,128},{256,192},{320,256},{384,320},{4... | collective-permute-start | bytes 589832 | tf_op jit(solution)/shard_map/ppermute | solution.py:21
  144.6 1.6 bitcast_dynamic-update-slice_fusion.6
  146.2 1.6 bitcast_dynamic-update-slice_fusion.5
  147.8 1.9 collective-permute-start.4
  149.7 5.1 %collective-permute-start.5 = (bf16[1,128,768]{2,1,0:T(8,128)(2,1)S(1)}, bf16[1,128,768]{2,1,0:T(8,128)(2,1)S(1)}, u32[]{:S(2)}, u32[]{:S(2)}) collective-permute-start(bf16[1,128,768]{2,1,0:T(8,128)(2,1)S(1)} %collective-permute-done.3), channel_id=1, source_target_pairs={{0,448},{64,0},{128,64},{192,128},{256,192},{320,256},{384,320},{4... | collective-permute-start | bytes 589832 | tf_op jit(solution)/shard_map/ppermute | solution.py:21
  154.9 0.7 bitcast_dynamic-update-slice_fusion.4
  155.6 0.7 bitcast_dynamic-update-slice_fusion.3
  156.2 0.4 collective-permute-done.4
  156.6 2.1 collective-permute-start.6
  158.7 0.7 bitcast_dynamic-update-slice_fusion.2
  159.4 0.7 bitcast_dynamic-update-slice_fusion.1
  160.1 5.3 %collective-permute-done.6 = bf16[1,128,768]{2,1,0:T(8,128)(2,1)S(1)} collective-permute-done((bf16[1,128,768]{2,1,0:T(8,128)(2,1)S(1)}, bf16[1,128,768]{2,1,0:T(8,128)(2,1)S(1)}, u32[]{:S(2)}, u32[]{:S(2)}) %collective-permute-start.6) | collective-permute-done | bytes 196640 | tf_op jit(solution)/shard_map/ppermute | solution.py:16
  165.4 0.7 bitcast_dynamic-update-slice_fusion
  166.1 5.6 %fusion.13 = f32[1024,768]{0,1:T(8,128)} fusion(bf16[1024,1024]{1,0:T(8,128)(2,1)} %bitcast.5, bf16[1024,768]{1,0:T(8,128)(2,1)} %bitcast_dynamic-update-slice_fusion), kind=kOutput, calls=%fused_computation.64 | convolution fusion | flops 1610612736 | bytes 6815744 | tf_op jit(solution)/shard_map/dot_general | solution.py:30
  171.7 5.0 %multiply_convert_fusion.1 = (bf16[1024,384]{0,1:T(8,128)(2,1)S(1)}, bf16[1024,384]{0,1:T(8,128)(2,1)S(1)}, bf16[1024,384]{0,1:T(8,128)(2,1)}) fusion(f32[1024,768]{0,1:T(8,128)} %fusion.13, bf16[1024,1024]{1,0:T(8,128)(2,1)S(1)} %bitcast.72, bf16[1,384,1024]{2,1,0:T(8,128)(2,1)S(1)} %all_gather.3), kind=kOutput, calls=%fused_computation.18 | convolution fusion | flops 811204608 | bytes 8388608 | tf_op jit(solution)/shard_map/dot_general | solution.py:44
  176.7 5.3 %convert_select_fusion = bf16[1024,1024]{1,0:T(8,128)(2,1)} fusion(pred[1024]{0:T(1024)(128)(4,1)S(1)} %lt.104, bf16[1024,768]{1,0:T(8,128)(2,1)} %bitcast_dynamic-update-slice_fusion, bf16[1024,384]{0,1:T(8,128)(2,1)S(1)} %get-tuple-element.25, bf16[1024,384]{0,1:T(8,128)(2,1)S(1)} %get-tuple-element.24), kind=kOutput, calls=%fused_computation.8 | convolution fusion | flops 1615855616 | bytes 5243904 | tf_op jit(solution)/shard_map/dot_general | solution.py:57
  182.1 10.1 %all-to-all-start.4 = ((bf16[64,16,1024]{2,1,0:T(8,128)(2,1)}), bf16[64,16,1024]{2,1,0:T(8,128)(2,1)S(1)}, u32[]{:S(2)}, u32[]{:S(2)}) async-start(bf16[64,16,1024]{2,1,0:T(8,128)(2,1)} %bitcast.75), calls=%async_computation.4 | async-start | bytes 4194304 | tf_op jit(solution)/shard_map/all_to_all | solution.py:133
  192.2 3.7 %fusion.4 = bf16[1,384,1024]{2,1,0:T(8,128)(2,1)} fusion(bf16[1024,384]{0,1:T(8,128)(2,1)} %get-tuple-element.26, bf16[1024,1024]{1,0:T(8,128)(2,1)} %bitcast.73), kind=kOutput, calls=%fused_computation.24 | convolution fusion | flops 805699584 | bytes 3670016 | tf_op jit(solution)/shard_map/dot_general | solution.py:63
  195.9 4.8 %copy.42 = bf16[1,384,1024]{1,0,2:T(2,128)(2,1)} copy(bf16[1,384,1024]{2,1,0:T(8,128)(2,1)} %fusion.4) | data formatting | bytes 1572864
  200.8 2.4 copy.48
  203.2 3.8 %convert_select_fusion.1 = bf16[1024,1024]{1,0:T(8,128)(2,1)} fusion(pred[1024]{0:T(1024)(128)(4,1)S(1)} %lt.104, bf16[1024,384]{0,1:T(8,128)(2,1)} %get-tuple-element.26, bf16[1,384,1024]{2,1,0:T(8,128)(2,1)S(1)} %all_gather.3), kind=kOutput, calls=%fused_computation.10 | convolution fusion | flops 807403520 | bytes 3671040 | tf_op jit(solution)/shard_map/dot_general | solution.py:34
  207.0 36.4 %all-to-all-done.4 = bf16[64,16,1024]{2,1,0:T(8,128)(2,1)S(1)} async-done(((bf16[64,16,1024]{2,1,0:T(8,128)(2,1)}), bf16[64,16,1024]{2,1,0:T(8,128)(2,1)S(1)}, u32[]{:S(2)}, u32[]{:S(2)}) %all-to-all-start.4) | async-done | bytes 2097184 | tf_op jit(solution)/shard_map/all_to_all | solution.py:133
  243.4 5.8 %all-to-all-start.2 = ((bf16[64,16,1024]{2,1,0:T(8,128)(2,1)}), bf16[64,16,1024]{2,1,0:T(8,128)(2,1)}, u32[]{:S(2)}, u32[]{:S(2)}) async-start(bf16[64,16,1024]{2,1,0:T(8,128)(2,1)} %bitcast.74), calls=%async_computation.2 | async-start | bytes 4194304 | tf_op jit(solution)/shard_map/all_to_all | solution.py:130
  249.2 0.3 reduce-scatter.5.cloned.1.call-start
  249.4 4.8 %fusion.3 = bf16[1,1024,768]{2,1,0:T(8,128)(2,1)} fusion(bf16[1024,1024]{1,0:T(8,128)(2,1)} %bitcast.5, bf16[1024,384]{0,1:T(8,128)(2,1)} %copy-done.7, bf16[1024,384]{0,1:T(8,128)(2,1)S(1)} %copy-done.6), kind=kOutput, calls=%fused_computation.22 | convolution fusion | flops 1614544896 | bytes 5242880 | tf_op jit(solution)/shard_map/dot_general | solution.py:60
  254.3 0.6 copy-done.3
  254.9 0.1 copy.39
  255.2 1.0 reshape_bitcast_fusion
  256.2 0.2 copy.43
  256.4 0.7 convert_element_type.81
  257.1 39.7 %reduce-scatter.5.cloned.1.call-done = bf16[1,128,768]{2,1,0:T(8,128)(2,1)} async-done(((bf16[1,1024,768]{2,1,0:T(8,128)(2,1)}), bf16[1,128,768]{2,1,0:T(8,128)(2,1)}) %reduce-scatter.5.cloned.1.call-update) | async-done | bytes 196624 | tf_op jit(solution)/shard_map/reduce_scatter | solution.py:135
  296.7 1.7 convert_element_type.78
  298.4 2.8 gather_fusion.4
  301.2 1.5 reshape.221
  302.7 2.1 reduce_sum.67
  304.8 5.3 %gather_fusion.1 = bf16[512,1024]{1,0:T(8,128)(2,1)} fusion(bf16[1024,1024]{1,0:T(8,128)(2,1)} %bitcast.16, s32[1024]{0:T(1024)S(1)} %pad_clamp_fusion), kind=kCustom, calls=%fused_computation.1 | custom fusion | bytes 2099200 | tf_op jit(solution)/shard_map/gather | solution.py:142
  310.1 1.7 reshape.222
  311.9 2.6 multiply_reduce_fusion
  314.4 0.7 copy.41
  (46 shorter events, 1.1 us)
Async XLA Ops:
  7.2 14.8 %copy-start = (bf16[128,1024]{1,0:T(8,128)(2,1)S(1)}, bf16[128,1024]{1,0:T(8,128)(2,1)}, u32[]{:S(2)}) copy-start(bf16[128,1024]{1,0:T(8,128)(2,1)} %param.6) | copy-start | bytes 786436
  10.6 19.2 %all-to-all-start = ((s32[64,1,1]{2,1,0:T(1,128)}), s32[64,1,1]{2,1,0:T(1,128)S(1)}, u32[]{:S(2)}, u32[]{:S(2)}) async-start(s32[64,1,1]{2,1,0:T(1,128)} %copy.36), calls=%async_computation | async-start | bytes 65536 | tf_op jit(solution)/shard_map/all_to_all | solution.py:126
  27.6 10.6 %copy-start.4 = (f32[128,4]{0,1:T(4,128)S(1)}, f32[128,4]{0,1:T(4,128)}, u32[]{:S(2)}) copy-start(f32[128,4]{0,1:T(4,128)} %param.8) | copy-start | bytes 6148
  29.8 59.6 %all-to-all-start.1 = ((bf16[64,16,1024]{2,1,0:T(8,128)(2,1)}), bf16[64,16,1024]{2,1,0:T(8,128)(2,1)}, u32[]{:S(2)}, u32[]{:S(2)}) async-start(bf16[64,16,1024]{2,1,0:T(8,128)(2,1)} %broadcast_select_fusion), calls=%async_computation.1 | async-start | bytes 4194304 | tf_op jit(solution)/shard_map/all_to_all | solution.py:125
  38.5 7.0 %copy-start.1 = (bf16[128,1024]{1,0:T(8,128)(2,1)S(1)}, bf16[128,1024]{1,0:T(8,128)(2,1)}, u32[]{:S(2)}) copy-start(bf16[128,1024]{1,0:T(8,128)(2,1)} %param.11) | copy-start | bytes 786436
  89.4 82.3 %all-to-all-start.3 = ((bf16[64,16,1024]{2,1,0:T(8,128)(2,1)}), bf16[64,16,1024]{2,1,0:T(8,128)(2,1)S(1)}, u32[]{:S(2)}, u32[]{:S(2)}) async-start(bf16[64,16,1024]{2,1,0:T(8,128)(2,1)} %fusion), calls=%async_computation.3 | async-start | bytes 4194304 | tf_op jit(solution)/shard_map/all_to_all | solution.py:131
  94.9 42.6 %collective-permute-start = (bf16[1,128,768]{2,1,0:T(8,128)(2,1)}, bf16[1,128,768]{2,1,0:T(8,128)(2,1)}, u32[]{:S(2)}, u32[]{:S(2)}) collective-permute-start(bf16[1,128,768]{2,1,0:T(8,128)(2,1)} %param.9), channel_id=1, source_target_pairs={{0,64},{64,128},{128,192},{192,256},{256,320},{320,384},{384,448},... | collective-permute-start | bytes 589832 | tf_op jit(solution)/shard_map/ppermute | solution.py:16
  99.1 40.6 %collective-permute-start.1 = (bf16[1,128,768]{2,1,0:T(8,128)(2,1)}, bf16[1,128,768]{2,1,0:T(8,128)(2,1)}, u32[]{:S(2)}, u32[]{:S(2)}) collective-permute-start(bf16[1,128,768]{2,1,0:T(8,128)(2,1)} %param.9), channel_id=1, source_target_pairs={{0,448},{64,0},{128,64},{192,128},{256,192},{320,256},{384,320},{4... | collective-permute-start | bytes 589832 | tf_op jit(solution)/shard_map/ppermute | solution.py:21
  137.5 10.3 %collective-permute-start.2 = (bf16[1,128,768]{2,1,0:T(8,128)(2,1)}, bf16[1,128,768]{2,1,0:T(8,128)(2,1)S(1)}, u32[]{:S(2)}, u32[]{:S(2)}) collective-permute-start(bf16[1,128,768]{2,1,0:T(8,128)(2,1)} %collective-permute-done), channel_id=1, source_target_pairs={{0,64},{64,128},{128,192},{192,256},{256,320},{320,384},{384,448},... | collective-permute-start | bytes 589832 | tf_op jit(solution)/shard_map/ppermute | solution.py:16
  139.7 10.0 %collective-permute-start.3 = (bf16[1,128,768]{2,1,0:T(8,128)(2,1)}, bf16[1,128,768]{2,1,0:T(8,128)(2,1)S(1)}, u32[]{:S(2)}, u32[]{:S(2)}) collective-permute-start(bf16[1,128,768]{2,1,0:T(8,128)(2,1)} %collective-permute-done.1), channel_id=1, source_target_pairs={{0,448},{64,0},{128,64},{192,128},{256,192},{320,256},{384,320},{4... | collective-permute-start | bytes 589832 | tf_op jit(solution)/shard_map/ppermute | solution.py:21
  147.8 8.8 %collective-permute-start.4 = (bf16[1,128,768]{2,1,0:T(8,128)(2,1)S(1)}, bf16[1,128,768]{2,1,0:T(8,128)(2,1)S(1)}, u32[]{:S(2)}, u32[]{:S(2)}) collective-permute-start(bf16[1,128,768]{2,1,0:T(8,128)(2,1)S(1)} %collective-permute-done.2), channel_id=1, source_target_pairs={{0,64},{64,128},{128,192},{192,256},{256,320},{320,384},{384,448},... | collective-permute-start | bytes 589832 | tf_op jit(solution)/shard_map/ppermute | solution.py:16
  149.7 9.7 %collective-permute-start.5 = (bf16[1,128,768]{2,1,0:T(8,128)(2,1)S(1)}, bf16[1,128,768]{2,1,0:T(8,128)(2,1)S(1)}, u32[]{:S(2)}, u32[]{:S(2)}) collective-permute-start(bf16[1,128,768]{2,1,0:T(8,128)(2,1)S(1)} %collective-permute-done.3), channel_id=1, source_target_pairs={{0,448},{64,0},{128,64},{192,128},{256,192},{320,256},{384,320},{4... | collective-permute-start | bytes 589832 | tf_op jit(solution)/shard_map/ppermute | solution.py:21
  156.6 8.8 %collective-permute-start.6 = (bf16[1,128,768]{2,1,0:T(8,128)(2,1)S(1)}, bf16[1,128,768]{2,1,0:T(8,128)(2,1)S(1)}, u32[]{:S(2)}, u32[]{:S(2)}) collective-permute-start(bf16[1,128,768]{2,1,0:T(8,128)(2,1)S(1)} %collective-permute-done.4), channel_id=1, source_target_pairs={{0,64},{64,128},{128,192},{192,256},{256,320},{320,384},{384,448},... | collective-permute-start | bytes 589832 | tf_op jit(solution)/shard_map/ppermute | solution.py:16
  171.7 5.0 %copy-start.2 = (bf16[64,16,1024]{2,1,0:T(8,128)(2,1)}, bf16[64,16,1024]{2,1,0:T(8,128)(2,1)S(1)}, u32[]{:S(2)}) copy-start(bf16[64,16,1024]{2,1,0:T(8,128)(2,1)S(1)} %all-to-all-done.3) | copy-start | bytes 6291460
  176.7 5.3 %copy-start.5 = (bf16[1024,384]{0,1:T(8,128)(2,1)}, bf16[1024,384]{0,1:T(8,128)(2,1)S(1)}, u32[]{:S(2)}) copy-start(bf16[1024,384]{0,1:T(8,128)(2,1)S(1)} %get-tuple-element.24) | copy-start | bytes 2359300
  176.7 5.3 %copy-start.7 = (bf16[1024,384]{0,1:T(8,128)(2,1)}, bf16[1024,384]{0,1:T(8,128)(2,1)S(1)}, u32[]{:S(2)}) copy-start(bf16[1024,384]{0,1:T(8,128)(2,1)S(1)} %get-tuple-element.25) | copy-start | bytes 2359300
  182.1 61.3 %all-to-all-start.4 = ((bf16[64,16,1024]{2,1,0:T(8,128)(2,1)}), bf16[64,16,1024]{2,1,0:T(8,128)(2,1)S(1)}, u32[]{:S(2)}, u32[]{:S(2)}) async-start(bf16[64,16,1024]{2,1,0:T(8,128)(2,1)} %bitcast.75), calls=%async_computation.4 | async-start | bytes 4194304 | tf_op jit(solution)/shard_map/all_to_all | solution.py:133
  192.2 63.0 %reduce-scatter.7.cloned.1.call-start = ((), (), s32[]{:S(2)}) async-start(), calls=%async_computation.8 | async-start | bytes 884736
  243.4 6.0 %copy-start.6 = (bf16[1024,384]{0,1:T(8,128)(2,1)S(1)}, bf16[1024,384]{0,1:T(8,128)(2,1)}, u32[]{:S(2)}) copy-start(bf16[1024,384]{0,1:T(8,128)(2,1)} %copy-done.5) | copy-start | bytes 2359300
  243.4 61.4 %all-to-all-start.2 = ((bf16[64,16,1024]{2,1,0:T(8,128)(2,1)}), bf16[64,16,1024]{2,1,0:T(8,128)(2,1)}, u32[]{:S(2)}, u32[]{:S(2)}) async-start(bf16[64,16,1024]{2,1,0:T(8,128)(2,1)} %bitcast.74), calls=%async_computation.2 | async-start | bytes 4194304 | tf_op jit(solution)/shard_map/all_to_all | solution.py:130
  249.2 47.6 %reduce-scatter.5.cloned.1.call-start = ((), (), s32[]{:S(2)}) async-start(), calls=%async_computation.7 | async-start | bytes 1769472 | tf_op jit(solution)/shard_map/reduce_scatter | solution.py:135
  254.2 0.7 copy-start.3
Sparse Core Ops, SparseCore 0:
  203.4 39.9 reduce-scatter.6
  254.4 42.3 reduce-scatter.4
